TPU v7x, 512 devices: a whole 4x8x8 slice. The times are simulated.
512 devices in a mesh: row: 4 (over y_hi), col: 16 (over y_lo, x, core), depth: 8 (over z).
Axes of the slice: x: 4, y: 8 (y_hi: 4, y_lo: 2; y = y_hi * 2 + y_lo), z: 8, core: 2. Of those that a mesh axis runs over, the one named last changes fastest.
Arguments:
- block_values: bfloat16 [32, 16, 16, 128, 128], P(('row', 'depth'), 'col'), may hold values from 0.0049743652 to 0.5
- block_cols: int32 [32, 16, 16], P(('row', 'depth'), 'col'), may hold values from 0 to 511, as said below
- live_count: int32 [32, 16], P(('row', 'depth'), 'col'), may hold values from 8 to 16, as said below
- out_pattern: int32 [4, 16, 32, 2], P('row', 'col'), may hold values from 0 to 511, as said below
Outputs:
- squared_log: bfloat16 [4, 16, 32, 128, 128], P('row', 'col', 'depth')
Inputs may be any that keep to these rules, and one draw needn't show every extreme that they name: Block row i's blocks are its first live_count slots; in every draw some block row is full. `block_cols`: the slots of one block row name distinct block columns. Call (k // 16) % 8 the depth part of a block index k and k // 32 its column group. Among the live slots of one block row at most 2 name a column in any one depth part and at most 2 in any one column group; both bounds are reached in every draw. The 32 entries of out_pattern[r, c] are distinct pairs (i, j) with i // 128 == r and j // 32 == c.
All inputs are finite; a program needn't handle non-finite values.
Results may differ from a plain program's by a relative error of at most 0.001.
Values may be sent and summed in bfloat16 or wider, within the bound.
No kernel may reach another device: no remote copies, remote signals or barrier semaphores. Data moves between devices by JAX's collectives and lax.ppermute only.
A program may use at most 128 MiB of HBM per device.

v0:
```python
import jax
import jax.numpy as jnp
from jax import lax
from jax.sharding import PartitionSpec as P


def pack_slots(values, col_ids, targets, is_live, part_count, capacity):
    row_count = col_ids.shape[0]
    block_size = values.shape[-1]
    chosen = (
        targets[:, :, None] == jnp.arange(part_count, dtype=jnp.int32)[None, None, :]
    ) & is_live[:, :, None]
    running = jnp.cumsum(chosen.astype(jnp.int32), axis=1) - 1
    order_in = jnp.sum(jnp.where(chosen, running, 0), axis=2)
    row_ids = jnp.arange(row_count, dtype=jnp.int32)[:, None]
    total = part_count * row_count * capacity
    position = (targets * row_count + row_ids) * capacity + order_in
    position = jnp.where(is_live, position, total).reshape(-1)
    packed = jnp.zeros((total, block_size, block_size), values.dtype)
    packed = packed.at[position].set(values.reshape(-1, block_size, block_size), mode="drop")
    return packed.reshape(part_count, row_count, capacity, block_size, block_size)


def body(block_values, block_cols, live_count, out_pattern):
    depths = lax.axis_size("depth")
    columns = lax.axis_size("col")
    row_groups = lax.axis_size("row")
    row_index = lax.axis_index("row")
    depth_index = lax.axis_index("depth")
    col_index = lax.axis_index("col")
    slot_count = block_values.shape[2]
    block_size = block_values.shape[3]
    group_rows = columns
    plane_rows = depths * group_rows
    col_block = row_groups * plane_rows // columns
    cap_left = slot_count // depths
    cap_right = 2
    values = block_values.reshape(1, slot_count, block_size, block_size)
    col_ids = block_cols.reshape(1, slot_count)
    counts = live_count.reshape(1)
    slots = jnp.arange(slot_count, dtype=jnp.int32)
    is_live = slots[None, :] < counts[:, None]
    meta = jnp.concatenate([col_ids, counts[:, None]], axis=1).astype(jnp.float32)
    meta = lax.all_gather(meta, ("row", "depth", "col"), axis=0, tiled=True).astype(jnp.int32)
    all_cols = meta[:, :slot_count]
    all_live = slots[None, :] < meta[:, slot_count:]
    left_vals = pack_slots(
        values, col_ids, col_ids // group_rows % depths, is_live, depths, cap_left
    )
    left_vals = lax.all_to_all(left_vals, "depth", split_axis=0, concat_axis=0, tiled=True)
    left_vals = lax.all_gather(left_vals[None], "col", axis=0, tiled=True)
    right_vals = pack_slots(values, col_ids, col_ids // col_block, is_live, columns, cap_right)
    right_vals = lax.all_to_all(right_vals, "col", split_axis=0, concat_axis=0, tiled=True)
    right_parts = [right_vals]
    for shift in range(1, row_groups):
        right_parts.append(
            lax.ppermute(
                right_vals,
                "row",
                perm=[(src, (src + shift) % row_groups) for src in range(row_groups)],
            )
        )
    right_flat = jnp.stack(right_parts).reshape(-1, block_size, block_size)
    pattern_rows = out_pattern[0, 0, :, 0]
    pattern_cols = out_pattern[0, 0, :, 1]
    pattern_len = pattern_rows.shape[0]
    local_row = pattern_rows - row_index * plane_rows
    left_pos = local_row % group_rows * depths + local_row // group_rows
    left_sel = left_pos[:, None] * cap_left + jnp.arange(cap_left, dtype=jnp.int32)[None, :]
    row_cols = jnp.take(all_cols, pattern_rows, axis=0)
    row_live = jnp.take(all_live, pattern_rows, axis=0)
    chosen = row_live & (row_cols // group_rows % depths == depth_index)
    rank = jnp.cumsum(chosen.astype(jnp.int32), axis=1) - 1
    picks = jnp.arange(cap_left, dtype=jnp.int32)
    hit = chosen[:, None, :] & (rank[:, None, :] == picks[None, :, None])
    has_inner = jnp.any(hit, axis=2)
    inner = jnp.sum(jnp.where(hit, row_cols[:, None, :], 0), axis=2)
    inner_cols = jnp.take(all_cols, inner, axis=0)
    inner_live = jnp.take(all_live, inner, axis=0)
    in_group = inner_live & (inner_cols // col_block == col_index)
    before = jnp.cumsum(in_group.astype(jnp.int32), axis=2) - 1
    match = in_group & (inner_cols == pattern_cols[:, None, None])
    found = jnp.any(match, axis=2) & has_inner
    slot = jnp.sum(jnp.where(match, before, 0), axis=2)
    shift_of = (row_index - inner // plane_rows) % row_groups
    right_row = shift_of * columns + inner % group_rows
    left_flat = left_vals.reshape(-1, block_size, block_size)
    left_pick = jnp.take(left_flat, left_sel.reshape(-1), axis=0)
    right_pick = jnp.take(right_flat, (right_row * cap_right + slot).reshape(-1), axis=0)
    right_pick = jnp.where(found.reshape(-1)[:, None, None], right_pick, jnp.zeros_like(right_pick))
    left_pick = left_pick.reshape(pattern_len, cap_left, block_size, block_size)
    right_pick = right_pick.reshape(pattern_len, cap_left, block_size, block_size)
    partial_sum = jnp.einsum(
        "pqab,pqbc->pac", left_pick, right_pick, preferred_element_type=jnp.float32
    )
    share = lax.psum_scatter(partial_sum[None, None], "depth", scatter_dimension=2, tiled=True)
    return jnp.log1p(share).astype(jnp.bfloat16)


def solution(mesh):
    in_specs = (
        P(("row", "depth"), "col", None, None, None),
        P(("row", "depth"), "col", None),
        P(("row", "depth"), "col"),
        P("row", "col", None, None),
    )
    out_specs = P("row", "col", "depth", None, None)
    return jax.shard_map(body, mesh=mesh, in_specs=in_specs, out_specs=out_specs, check_vma=False)
```

profile of v0, /device:TPU:12, one launch (start us, length us, event | category | flops | bytes accessed | tf_op | source)
XLA Modules:
  0.0 870.1 jit_solution(6802126021564995380)
XLA Ops:
  6.5 0.0 all-gather.4.cloned.1.call-start
  7.2 0.7 and_select_fusion.8
  7.9 0.1 fusion.26
  8.0 0.2 select_reduce_fusion.3
  8.2 0.1 fusion.28
  8.3 0.2 select_reduce_fusion.2
  8.5 0.7 fusion.41
  9.2 0.1 broadcast_in_dim.119
  9.3 0.0 copy-start
  9.3 2.1 scatter_fusion
  11.3 27.7 %all_to_all.10 = bf16[8,1,2,128,128]{4,3,2,1,0:T(8,128)(2,1)} all-to-all(bf16[8,1,2,128,128]{4,3,2,1,0:T(8,128)(2,1)S(1)} %bitcast.99), channel_id=1, replica_groups=mesh['row'=4,'col'=16,'depth'=8] {'depth'}, dimensions={0} | all-to-all | bytes 1048576 | tf_op jit(solution)/shard_map/all_to_all | solution.py:50
  39.1 0.0 all-gather.4.cloned.1.call-update
  39.1 1.3 broadcast_in_dim.133
  40.4 0.0 copy-done
  40.4 0.0 copy-start.1
  40.4 0.0 copy-start.2
  40.4 2.6 scatter_fusion.1
  43.0 5.7 all-to-all-start.1
  48.7 0.0 reduce-scatter.2.cloned.1.call-start
  48.8 0.0 copy-done.1
  48.8 0.1 fusion.46
  48.9 668.3 %all-gather.1 = f32[512,1,17]{2,1,0:T(1,128)S(1)} all-gather(f32[1,1,17]{2,1,0:T(1,128)S(1)} %fusion.46), channel_id=1, replica_groups=mesh['row'=4,'col'=16,'depth'=8] {'row','depth','col'}, dimensions={0}, use_global_device_ids=true | all-gather | bytes 34884 | tf_op jit(solution)/shard_map/all_gather | solution.py:44
  717.1 0.0 copy-done.2
  717.2 0.6 gather_fusion.2
  717.8 0.2 slice_reduce_fusion
  718.0 0.1 iota_compare_fusion
  718.1 0.6 gather_fusion.1
  718.7 0.1 fusion.52
  718.8 0.2 reduce_window_sum.45
  719.0 0.1 broadcast_add_fusion
  719.1 0.1 select_reduce_fusion.1
  719.2 0.1 copy.18
  719.3 0.1 reshape.1156
  719.4 0.6 gather_fusion.4
  720.0 0.6 gather_fusion.3
  720.8 0.2 fusion.50
  721.0 0.0 all-to-all-done.1
  721.0 6.9 collective-permute-start.1
  727.9 1.9 collective-permute-start
  729.8 6.0 collective-permute-start.2
  735.8 0.1 fusion.17
  735.9 0.1 copy.25
  736.0 0.1 copy.15
  736.1 0.1 copy.16
  736.2 0.1 add.385
  736.3 0.1 copy.21
  736.5 0.1 reduce_sum.53
  736.6 0.4 reduce_window_sum.46
  736.9 0.1 select_reduce_fusion
  737.1 0.1 copy.26
  737.2 0.1 copy.22
  737.3 0.1 reduce_sum.54
  737.5 15.5 %collective-permute-done.1 = bf16[16,1,2,128,128]{4,3,2,0,1:T(8,128)(2,1)S(1)} collective-permute-done((bf16[16,1,2,128,128]{4,3,2,0,1:T(8,128)(2,1)S(1)}, bf16[16,1,2,128,128]{4,3,2,0,1:T(8,128)(2,1)S(1)}, u32[]{:S(2)}, u32[]{:S(2)}) %collective-permute-start.1) | collective-permute-done | bytes 1048608 | tf_op jit(solution)/shard_map/ppermute | solution.py:57
  753.0 48.9 %collective-permute-done = bf16[16,1,2,128,128]{4,3,2,0,1:T(8,128)(2,1)S(1)} collective-permute-done((bf16[16,1,2,128,128]{4,3,2,0,1:T(8,128)(2,1)S(1)}, bf16[16,1,2,128,128]{4,3,2,0,1:T(8,128)(2,1)S(1)}, u32[]{:S(2)}, u32[]{:S(2)}) %collective-permute-start) | collective-permute-done | bytes 1048608 | tf_op jit(solution)/shard_map/ppermute | solution.py:57
  801.9 0.0 collective-permute-done.2
  801.9 3.3 pad_maximum_fusion
  805.2 3.1 gather_fusion.5
  808.3 0.0 all-gather.4.cloned.1.call-done
  808.3 5.6 gather_fusion
  813.9 3.7 fusion.7
  817.7 0.0 reduce-scatter.2.cloned.1.call-update
  817.7 43.8 %reduce-scatter.2.cloned.1.call-done = f32[1,1,4,128,128]{4,3,2,1,0:T(8,128)} async-done(((f32[1,1,32,128,128]{4,3,2,1,0:T(8,128)}), f32[1,1,4,128,128]{4,3,2,1,0:T(8,128)}) %reduce-scatter.2.cloned.1.call-update) | async-done | bytes 262160 | tf_op jit(solution)/shard_map/reduce_scatter | solution.py:96
  861.5 1.7 log-plus-one_convert_fusion
  (22 shorter events, 0.3 us)
Async XLA Ops:
  6.5 801.8 %all-gather.4.cloned.1.call-start = ((), (), s32[]{:S(2)}) async-start(), calls=%async_computation.4 | async-start | bytes 8912896 | tf_op jit(solution)/shard_map/all_gather | solution.py:51
  9.3 31.1 %copy-start = (bf16[1,1,16,128,128]{4,3,2,1,0:T(8,128)(2,1)S(1)}, bf16[1,1,16,128,128]{4,3,2,1,0:T(8,128)(2,1)}, u32[]{:S(2)}) copy-start(bf16[1,1,16,128,128]{4,3,2,1,0:T(8,128)(2,1)} %param.4) | copy-start | bytes 1572868
  40.4 8.4 copy-start.1
  40.4 676.7 %copy-start.2 = (s32[1,1,32,2]{2,3,1,0:T(2,128)S(1)}, s32[1,1,32,2]{2,3,1,0:T(2,128)}, u32[]{:S(2)}) copy-start(s32[1,1,32,2]{2,3,1,0:T(2,128)} %param.7) | copy-start | bytes 772
  43.0 678.0 %all-to-all-start.1 = ((bf16[16,1,2,128,128]{4,3,2,1,0:T(8,128)(2,1)}), bf16[16,1,2,128,128]{4,3,2,1,0:T(8,128)(2,1)S(1)}, u32[]{:S(2)}, u32[]{:S(2)}) async-start(bf16[16,1,2,128,128]{4,3,2,1,0:T(8,128)(2,1)} %bitcast.22), calls=%async_computation.1 | async-start | bytes 2097152 | tf_op jit(solution)/shard_map/all_to_all | solution.py:53
  48.7 812.8 %reduce-scatter.2.cloned.1.call-start = ((), (), s32[]{:S(2)}) async-start(), calls=%async_computation.3 | async-start | bytes 2359296 | tf_op jit(solution)/shard_map/reduce_scatter | solution.py:96
  721.0 32.0 %collective-permute-start.1 = (bf16[16,1,2,128,128]{4,3,2,0,1:T(8,128)(2,1)S(1)}, bf16[16,1,2,128,128]{4,3,2,0,1:T(8,128)(2,1)S(1)}, u32[]{:S(2)}, u32[]{:S(2)}) collective-permute-start(bf16[16,1,2,128,128]{4,3,2,0,1:T(8,128)(2,1)S(1)} %bitcast.100), channel_id=1, source_target_pairs={{0,256},{128,384},{256,0},{384,128},{1,257},{129,385},{257,1},{385... | collective-permute-start | bytes 3145736 | tf_op jit(solution)/shard_map/ppermute | solution.py:57
  727.9 74.0 %collective-permute-start = (bf16[16,1,2,128,128]{4,3,2,0,1:T(8,128)(2,1)S(1)}, bf16[16,1,2,128,128]{4,3,2,0,1:T(8,128)(2,1)S(1)}, u32[]{:S(2)}, u32[]{:S(2)}) collective-permute-start(bf16[16,1,2,128,128]{4,3,2,0,1:T(8,128)(2,1)S(1)} %bitcast.101), channel_id=1, source_target_pairs={{0,128},{128,256},{256,384},{384,0},{1,129},{129,257},{257,385},{3... | collective-permute-start | bytes 3145736 | tf_op jit(solution)/shard_map/ppermute | solution.py:57
  729.8 72.1 %collective-permute-start.2 = (bf16[16,1,2,128,128]{4,3,2,1,0:T(8,128)(2,1)S(1)}, bf16[16,1,2,128,128]{4,3,2,1,0:T(8,128)(2,1)}, u32[]{:S(2)}, u32[]{:S(2)}) collective-permute-start(bf16[16,1,2,128,128]{4,3,2,1,0:T(8,128)(2,1)S(1)} %all-to-all-done.1), channel_id=1, source_target_pairs={{0,384},{128,0},{256,128},{384,256},{1,385},{129,1},{257,129},{385... | collective-permute-start | bytes 3145736 | tf_op jit(solution)/shard_map/ppermute | solution.py:57
Sparse Core Ops, SparseCore 0:
  39.2 64.2 all-gather.3
  817.8 43.6 reduce-scatter.1
where the time goes:
time: 871 us; the launch traced here: 870 us
  blocking collectives  696 us (80%)
  waiting for transfers between devices  108 us (12%)
  starting transfers between devices  20.6 us (2%)
  local copies, waits for them, and re-layouts  18.6 us (2%)
  between operations  14.3 us (2%)
    all_gather x1, blocking collectives, body(): lax.all_gather(meta, ('row', 'depth', 'col'), axis=0, tiled=True)  668 us
    ppermute x3, waiting for transfers between devices, body(): lax.ppermute(right_vals, 'row', perm=[(src, (src + shift) % row_groups) f...  64.4 us
    reduce_scatter x1, waiting for transfers between devices, body(): lax.psum_scatter(partial_sum[None, None], 'depth', scatter_dimension=2, t...  43.8 us
    all_to_all x1, blocking collectives, body(): lax.all_to_all(left_vals, 'depth', split_axis=0, concat_axis=0, tiled=True)  27.7 us
  transfers between devices with their start and end apart: 6, of which 3 were waited for; matrix products, arithmetic and copies ran while one was open for 2% of the time, Pallas kernels for 0%

commit v1 on v0

--- a/solution.py
+++ b/solution.py
@@ -1,7 +1,18 @@
+import functools
 import jax
 import jax.numpy as jnp
 from jax import lax
 from jax.sharding import PartitionSpec as P
+
+
+def cover_ladders(a0, mesh_ax):
+    o_now = tuple((a0 for _ in range(jax.lax.axis_size(mesh_ax))))
+    small = jnp.stack(o_now, axis=0)
+    carry_in = jax.lax.all_to_all(small, mesh_ax, 0, 0)
+    return jnp.concatenate(carry_in, axis=0)
+
+
+tokens_reach = functools.partial(cover_ladders, mesh_ax=("row", "depth", "col"))
 
 
 def pack_slots(values, col_ids, targets, is_live, part_count, capacity):
@@ -41,7 +52,7 @@
     slots = jnp.arange(slot_count, dtype=jnp.int32)
     is_live = slots[None, :] < counts[:, None]
     meta = jnp.concatenate([col_ids, counts[:, None]], axis=1).astype(jnp.float32)
-    meta = lax.all_gather(meta, ("row", "depth", "col"), axis=0, tiled=True).astype(jnp.int32)
+    meta = tokens_reach(meta).astype(jnp.int32)
     all_cols = meta[:, :slot_count]
     all_live = slots[None, :] < meta[:, slot_count:]
     left_vals = pack_slots(

time: 871 us -> 269 us (0.31)
  the two profiles are of different devices: /device:TPU:12 before, /device:TPU:4 now
where the time goes in v1:
time: 269 us
  waiting for transfers between devices  166 us (62%)
  starting transfers between devices  28.6 us (11%)
  blocking collectives  27.9 us (10%)
  local copies, waits for them, and re-layouts  19.4 us (7%)
  between operations  14.3 us (5%)
  other arithmetic  8.6 us (3%)
  matrix products  3.74 us (1%)
    ppermute x3, waiting for transfers between devices, body(): lax.ppermute(right_vals, 'row', perm=[(src, (src + shift) % row_groups) f...  82.5 us
    reduce_scatter x1, waiting for transfers between devices, body(): lax.psum_scatter(partial_sum[None, None], 'depth', scatter_dimension=2, t...  49.6 us
    all_to_all x1, blocking collectives, body(): lax.all_to_all(left_vals, 'depth', split_axis=0, concat_axis=0, tiled=True)  27.9 us
    all_to_all x1, waiting for transfers between devices, body(): lax.all_to_all(right_vals, 'col', split_axis=0, concat_axis=0, tiled=True)  19.7 us
    all_to_all x1, waiting for transfers between devices, cover_ladders(): carry_in = jax.lax.all_to_all(small, mesh_ax, 0, 0)  14.3 us
    all_to_all x1, starting transfers between devices, cover_ladders(): carry_in = jax.lax.all_to_all(small, mesh_ax, 0, 0)  12.7 us
    ppermute x3, starting transfers between devices, body(): lax.ppermute(right_vals, 'row', perm=[(src, (src + shift) % row_groups) f...  10.9 us
    gather x1, local copies, waits for them, and re-layouts, body(): left_pick = jnp.take(left_flat, left_sel.reshape(-1), axis=0)  5.59 us
  transfers between devices with their start and end apart: 7, of which 6 were waited for; matrix products, arithmetic and copies ran while one was open for 6% of the time, Pallas kernels for 0%

profile of v1, /device:TPU:4, one launch (start us, length us, event | category | flops | bytes accessed | tf_op | source)
XLA Modules:
  0.0 268.6 jit_solution(8016768821458796365)
XLA Ops:
  6.5 0.0 all-gather.3.cloned.1.call-start
  7.2 0.7 and_select_fusion.8
  7.9 0.1 fusion.26
  8.0 0.2 select_reduce_fusion.3
  8.2 0.1 fusion.28
  8.3 0.2 select_reduce_fusion.2
  8.5 0.7 fusion.41
  9.2 0.1 broadcast_in_dim.119
  9.3 0.0 copy-start.2
  9.3 2.1 scatter_fusion
  11.4 0.0 copy-start
  11.4 27.9 %all_to_all.15 = bf16[8,1,2,128,128]{4,3,2,1,0:T(8,128)(2,1)} all-to-all(bf16[8,1,2,128,128]{4,3,2,1,0:T(8,128)(2,1)S(1)} %bitcast.86), channel_id=1, replica_groups=mesh['row'=4,'col'=16,'depth'=8] {'depth'}, dimensions={0} | all-to-all | bytes 1048576 | tf_op jit(solution)/shard_map/all_to_all | solution.py:61
  39.2 0.0 all-gather.3.cloned.1.call-update
  39.3 0.0 copy-done.1
  39.3 0.1 add_convert_fusion
  39.3 0.8 stack.12
  40.2 12.7 %all-to-all-start.1 = ((f32[512,1,17]{2,1,0:T(1,128)}), f32[512,1,17]{2,1,0:T(1,128)S(1)}, u32[]{:S(2)}, u32[]{:S(2)}) async-start(f32[512,1,17]{2,1,0:T(1,128)} %stack.12), calls=%async_computation.1 | async-start | bytes 524288 | tf_op jit(solution)/shard_map/all_to_all | solution.py:11
  52.9 0.0 copy-done.2
  52.9 0.1 copy.14
  53.0 0.1 add.385
  53.2 1.3 broadcast_in_dim.133
  54.5 0.0 copy-done
  54.5 2.6 scatter_fusion.1
  57.1 14.3 %all-to-all-done.1 = f32[512,1,17]{2,1,0:T(1,128)S(1)} async-done(((f32[512,1,17]{2,1,0:T(1,128)}), f32[512,1,17]{2,1,0:T(1,128)S(1)}, u32[]{:S(2)}, u32[]{:S(2)}) %all-to-all-start.1) | async-done | bytes 34848 | tf_op jit(solution)/shard_map/all_to_all | solution.py:11
  71.4 4.9 %all-to-all-start.2 = ((bf16[16,1,2,128,128]{4,3,2,1,0:T(8,128)(2,1)}), bf16[16,1,2,128,128]{4,3,2,1,0:T(8,128)(2,1)S(1)}, u32[]{:S(2)}, u32[]{:S(2)}) async-start(bf16[16,1,2,128,128]{4,3,2,1,0:T(8,128)(2,1)} %bitcast.21), calls=%async_computation.2 | async-start | bytes 2097152 | tf_op jit(solution)/shard_map/all_to_all | solution.py:64
  76.3 0.0 reduce-scatter.2.cloned.1.call-start
  76.4 0.1 copy.13
  76.5 0.6 gather_fusion.2
  77.1 0.2 slice_reduce_fusion
  77.3 0.1 iota_compare_fusion
  77.5 0.6 gather_fusion.1
  78.1 0.1 fusion.51
  78.2 0.2 reduce_window_sum.45
  78.3 0.1 broadcast_add_fusion
  78.4 0.1 select_reduce_fusion.1
  78.5 0.1 copy.16
  78.6 0.1 reshape.1156
  78.8 19.7 %all-to-all-done.2 = bf16[16,1,2,128,128]{4,3,2,1,0:T(8,128)(2,1)S(1)} async-done(((bf16[16,1,2,128,128]{4,3,2,1,0:T(8,128)(2,1)}), bf16[16,1,2,128,128]{4,3,2,1,0:T(8,128)(2,1)S(1)}, u32[]{:S(2)}, u32[]{:S(2)}) %all-to-all-start.2) | async-done | bytes 1048608 | tf_op jit(solution)/shard_map/all_to_all | solution.py:64
  98.4 3.0 %collective-permute-start.1 = (bf16[16,1,2,128,128]{4,3,2,0,1:T(8,128)(2,1)S(1)}, bf16[16,1,2,128,128]{4,3,2,0,1:T(8,128)(2,1)S(1)}, u32[]{:S(2)}, u32[]{:S(2)}) collective-permute-start(bf16[16,1,2,128,128]{4,3,2,0,1:T(8,128)(2,1)S(1)} %bitcast.87), channel_id=1, source_target_pairs={{0,256},{128,384},{256,0},{384,128},{1,257},{129,385},{257,1},{385... | collective-permute-start | bytes 3145736 | tf_op jit(solution)/shard_map/ppermute | solution.py:68
  101.4 4.4 %collective-permute-start = (bf16[16,1,2,128,128]{4,3,2,0,1:T(8,128)(2,1)S(1)}, bf16[16,1,2,128,128]{4,3,2,0,1:T(8,128)(2,1)S(1)}, u32[]{:S(2)}, u32[]{:S(2)}) collective-permute-start(bf16[16,1,2,128,128]{4,3,2,0,1:T(8,128)(2,1)S(1)} %bitcast.88), channel_id=1, source_target_pairs={{0,128},{128,256},{256,384},{384,0},{1,129},{129,257},{257,385},{3... | collective-permute-start | bytes 3145736 | tf_op jit(solution)/shard_map/ppermute | solution.py:68
  105.9 3.5 %collective-permute-start.2 = (bf16[16,1,2,128,128]{4,3,2,1,0:T(8,128)(2,1)S(1)}, bf16[16,1,2,128,128]{4,3,2,1,0:T(8,128)(2,1)}, u32[]{:S(2)}, u32[]{:S(2)}) collective-permute-start(bf16[16,1,2,128,128]{4,3,2,1,0:T(8,128)(2,1)S(1)} %all-to-all-done.2), channel_id=1, source_target_pairs={{0,384},{128,0},{256,128},{384,256},{1,385},{129,1},{257,129},{385... | collective-permute-start | bytes 3145736 | tf_op jit(solution)/shard_map/ppermute | solution.py:68
  109.4 0.6 gather_fusion.4
  110.0 0.6 gather_fusion.3
  110.6 0.1 copy.23
  110.7 0.1 fusion.17
  110.9 0.2 fusion.49
  111.1 0.1 copy.19
  111.2 0.1 reduce_sum.53
  111.3 0.4 reduce_window_sum.46
  111.7 0.1 select_reduce_fusion
  111.8 0.1 copy.24
  111.9 0.1 copy.20
  112.0 0.1 reduce_sum.54
  112.2 33.8 %collective-permute-done.1 = bf16[16,1,2,128,128]{4,3,2,0,1:T(8,128)(2,1)S(1)} collective-permute-done((bf16[16,1,2,128,128]{4,3,2,0,1:T(8,128)(2,1)S(1)}, bf16[16,1,2,128,128]{4,3,2,0,1:T(8,128)(2,1)S(1)}, u32[]{:S(2)}, u32[]{:S(2)}) %collective-permute-start.1) | collective-permute-done | bytes 1048608 | tf_op jit(solution)/shard_map/ppermute | solution.py:68
  146.0 27.4 %collective-permute-done = bf16[16,1,2,128,128]{4,3,2,0,1:T(8,128)(2,1)S(1)} collective-permute-done((bf16[16,1,2,128,128]{4,3,2,0,1:T(8,128)(2,1)S(1)}, bf16[16,1,2,128,128]{4,3,2,0,1:T(8,128)(2,1)S(1)}, u32[]{:S(2)}, u32[]{:S(2)}) %collective-permute-start) | collective-permute-done | bytes 1048608 | tf_op jit(solution)/shard_map/ppermute | solution.py:68
  173.4 21.3 %collective-permute-done.2 = bf16[16,1,2,128,128]{4,3,2,1,0:T(8,128)(2,1)} collective-permute-done((bf16[16,1,2,128,128]{4,3,2,1,0:T(8,128)(2,1)S(1)}, bf16[16,1,2,128,128]{4,3,2,1,0:T(8,128)(2,1)}, u32[]{:S(2)}, u32[]{:S(2)}) %collective-permute-start.2) | collective-permute-done | bytes 1048608 | tf_op jit(solution)/shard_map/ppermute | solution.py:68
  194.7 3.3 %pad_maximum_fusion = bf16[4,16,1,2,128,128]{5,4,3,1,2,0:T(8,128)(2,1)} fusion(bf16[1,16,1,2,128,128]{5,4,3,1,2,0:T(8,128)(2,1)} %bitcast.27, bf16[1,16,1,2,128,128]{5,4,3,1,2,0:T(8,128)(2,1)S(1)} %bitcast.97, bf16[1,16,1,2,128,128]{5,4,3,1,2,0:T(8,128)(2,1)S(1)} %bitcast.98, bf16[1,16,1,2,128,128]{5,4,3,1,2,0:T(8,128)(2,1)S(1)} %bitcast.89), kind=kLoop, calls=%fused_computation.8 | loop fusion | flops 6291456 | bytes 8388608 | tf_op jit(solution)/shard_map/stack | solution.py:74
  198.0 3.1 %gather_fusion.5 = bf16[64,128,128]{2,1,0:T(8,128)(2,1)S(1)} fusion(bf16[128,128,128]{2,1,0:T(8,128)(2,1)} %bitcast.85, s32[1024]{0:T(1024)S(1)} %pad_clamp_fusion), kind=kCustom, calls=%fused_computation.5 | custom fusion | bytes 4194560 | tf_op jit(solution)/shard_map/jit(_take)/gather | solution.py:100
  201.1 0.0 all-gather.3.cloned.1.call-done
  201.2 5.6 %gather_fusion = bf16[64,128,128]{2,1,0:T(8,128)(2,1)} fusion(bf16[256,128,128]{2,1,0:T(8,128)(2,1)} %bitcast.99, s32[1024]{0:T(1024)S(1)} %pad_clamp_fusion.3), kind=kCustom, calls=%fused_computation | custom fusion | bytes 4194560 | tf_op jit(solution)/shard_map/jit(_take)/gather | solution.py:99
  206.8 3.7 %fusion.7 = f32[1,1,32,128,128]{4,3,2,1,0:T(8,128)} fusion(bf16[32,2,128,128]{3,2,1,0:T(8,128)(2,1)S(1)} %bitcast.92, pred[32,2]{1,0:T(8,128)(4,1)S(1)} %copy.20, pred[32,2]{1,0:T(8,128)(4,1)S(1)} %copy.19, bf16[32,2,128,128]{3,2,1,0:T(8,128)(2,1)} %bitcast.93, pred[32,2]{1,0:T(8,128)(4,1)S(1)} %copy.13), kind=kOutput, calls=%fused_computation.16 | convolution fusion | flops 271581184 | bytes 6291648 | tf_op jit(solution)/shard_map/pqab,pqbc->pac/dot_general | solution.py:104
  210.5 0.0 reduce-scatter.2.cloned.1.call-update
  210.5 49.6 %reduce-scatter.2.cloned.1.call-done = f32[1,1,4,128,128]{4,3,2,1,0:T(8,128)} async-done(((f32[1,1,32,128,128]{4,3,2,1,0:T(8,128)}), f32[1,1,4,128,128]{4,3,2,1,0:T(8,128)}) %reduce-scatter.2.cloned.1.call-update) | async-done | bytes 262160 | tf_op jit(solution)/shard_map/reduce_scatter | solution.py:107
  260.1 1.7 log-plus-one_convert_fusion
  (23 shorter events, 0.3 us)
Async XLA Ops:
  6.5 32.7 %copy-start.1 = (s32[1,1,16]{2,1,0:T(1,128)S(1)}, s32[1,1,16]{2,1,0:T(1,128)}, u32[]{:S(2)}) copy-start(s32[1,1,16]{2,1,0:T(1,128)} %param.5) | copy-start | bytes 196
  6.5 194.6 %all-gather.3.cloned.1.call-start = ((), (), s32[]{:S(2)}) async-start(), calls=%async_computation.5 | async-start | bytes 8912896 | tf_op jit(solution)/shard_map/all_gather | solution.py:62
  9.3 43.6 %copy-start.2 = (s32[1,1,32,2]{2,3,1,0:T(2,128)S(1)}, s32[1,1,32,2]{2,3,1,0:T(2,128)}, u32[]{:S(2)}) copy-start(s32[1,1,32,2]{2,3,1,0:T(2,128)} %param.7) | copy-start | bytes 772
  11.4 43.1 %copy-start = (bf16[1,1,16,128,128]{4,3,2,1,0:T(8,128)(2,1)S(1)}, bf16[1,1,16,128,128]{4,3,2,1,0:T(8,128)(2,1)}, u32[]{:S(2)}) copy-start(bf16[1,1,16,128,128]{4,3,2,1,0:T(8,128)(2,1)} %param.4) | copy-start | bytes 1572868
  40.2 31.2 %all-to-all-start.1 = ((f32[512,1,17]{2,1,0:T(1,128)}), f32[512,1,17]{2,1,0:T(1,128)S(1)}, u32[]{:S(2)}, u32[]{:S(2)}) async-start(f32[512,1,17]{2,1,0:T(1,128)} %stack.12), calls=%async_computation.1 | async-start | bytes 524288 | tf_op jit(solution)/shard_map/all_to_all | solution.py:11
  71.4 27.0 %all-to-all-start.2 = ((bf16[16,1,2,128,128]{4,3,2,1,0:T(8,128)(2,1)}), bf16[16,1,2,128,128]{4,3,2,1,0:T(8,128)(2,1)S(1)}, u32[]{:S(2)}, u32[]{:S(2)}) async-start(bf16[16,1,2,128,128]{4,3,2,1,0:T(8,128)(2,1)} %bitcast.21), calls=%async_computation.2 | async-start | bytes 2097152 | tf_op jit(solution)/shard_map/all_to_all | solution.py:64
  76.3 183.8 %reduce-scatter.2.cloned.1.call-start = ((), (), s32[]{:S(2)}) async-start(), calls=%async_computation.4 | async-start | bytes 2359296 | tf_op jit(solution)/shard_map/reduce_scatter | solution.py:107
  98.4 47.6 %collective-permute-start.1 = (bf16[16,1,2,128,128]{4,3,2,0,1:T(8,128)(2,1)S(1)}, bf16[16,1,2,128,128]{4,3,2,0,1:T(8,128)(2,1)S(1)}, u32[]{:S(2)}, u32[]{:S(2)}) collective-permute-start(bf16[16,1,2,128,128]{4,3,2,0,1:T(8,128)(2,1)S(1)} %bitcast.87), channel_id=1, source_target_pairs={{0,256},{128,384},{256,0},{384,128},{1,257},{129,385},{257,1},{385... | collective-permute-start | bytes 3145736 | tf_op jit(solution)/shard_map/ppermute | solution.py:68
  101.4 72.0 %collective-permute-start = (bf16[16,1,2,128,128]{4,3,2,0,1:T(8,128)(2,1)S(1)}, bf16[16,1,2,128,128]{4,3,2,0,1:T(8,128)(2,1)S(1)}, u32[]{:S(2)}, u32[]{:S(2)}) collective-permute-start(bf16[16,1,2,128,128]{4,3,2,0,1:T(8,128)(2,1)S(1)} %bitcast.88), channel_id=1, source_target_pairs={{0,128},{128,256},{256,384},{384,0},{1,129},{129,257},{257,385},{3... | collective-permute-start | bytes 3145736 | tf_op jit(solution)/shard_map/ppermute | solution.py:68
  105.9 88.8 %collective-permute-start.2 = (bf16[16,1,2,128,128]{4,3,2,1,0:T(8,128)(2,1)S(1)}, bf16[16,1,2,128,128]{4,3,2,1,0:T(8,128)(2,1)}, u32[]{:S(2)}, u32[]{:S(2)}) collective-permute-start(bf16[16,1,2,128,128]{4,3,2,1,0:T(8,128)(2,1)S(1)} %all-to-all-done.2), channel_id=1, source_target_pairs={{0,384},{128,0},{256,128},{384,256},{1,385},{129,1},{257,129},{385... | collective-permute-start | bytes 3145736 | tf_op jit(solution)/shard_map/ppermute | solution.py:68
Sparse Core Ops, SparseCore 0:
  39.4 69.3 all-gather.2
  210.6 49.3 reduce-scatter.1
